TPU v7x, 256 devices: a whole 4x4x8 slice. The times are simulated.
256 devices in a mesh: row: 4 (over y), col: 64 (over z, x, core).
Axes of the slice: x: 4, y: 4, z: 8, core: 2. Of those that a mesh axis runs over, the one named last changes fastest.
Arguments:
- tokens: bfloat16 [32768, 4096], P(('row', 'col')), may hold values from -6 to 6
- expert_ids: int32 [32768, 2], P(('row', 'col')), may hold values from 0 to 63, all different within a row; in each aligned block of 128 rows (0 to 127, 128 to 255, ...) at most 5 rows name the same one
- gate_weights: float32 [32768, 2], P(('row', 'col')), may hold values from 0.1 to 1
- w_gate: bfloat16 [64, 4096, 1536], P('col', None, 'row'), may hold values from -0.09375 to 0.09375
- w_up: bfloat16 [64, 4096, 1536], P('col', None, 'row'), may hold values from -0.09375 to 0.09375
- w_down: bfloat16 [64, 1536, 4096], P('col', None, 'row'), may hold values from -0.15625 to 0.15625
Outputs:
- moe_out: bfloat16 [32768, 4096], P(('row', 'col'))
Inputs may be any that keep to these rules, and one draw needn't show every extreme that they name: `expert_ids`: each row names 2 different experts. Among the 128 rows of one device no expert is named by more than 5 rows, and in every draw some expert is named by exactly 5 rows of some device.
All inputs are finite; a program needn't handle non-finite values.
Results may differ from a plain program's by a relative error of at most 0.0058.
Values may be sent and summed in bfloat16 or wider, within the bound.
No kernel may reach another device: no remote copies, remote signals or barrier semaphores. Data moves between devices by JAX's collectives and lax.ppermute only.
A program may use at most 128 MiB of HBM per device.

v0:
```python
import jax
import jax.numpy as jnp
from jax import lax
from jax.sharding import PartitionSpec as P


def local(tokens, expert_ids, gate_weights, w_gate, w_up, w_down):
    token_count, top_count = expert_ids.shape
    width = tokens.shape[1]
    local_count = w_gate.shape[0]
    unit_count = w_gate.shape[2]
    quarter = w_down.shape[2]
    columns = lax.axis_size("col")
    groups = lax.axis_size("row")
    experts = local_count * columns
    capacity = max(2, token_count * top_count * 5 // (4 * experts))
    flat_ids = expert_ids.reshape(-1)
    onehot = (flat_ids[:, None] == jnp.arange(experts, dtype=jnp.int32)[None, :]).astype(jnp.int32)
    earlier = jnp.cumsum(onehot, axis=0) - onehot
    position = jnp.sum(earlier * onehot, axis=1)
    slot_ids = (flat_ids * capacity + position).reshape(token_count, top_count)
    chooser = jnp.any(
        jnp.arange(experts * capacity, dtype=jnp.int32)[:, None, None] == slot_ids[None, :, :],
        axis=2,
    ).astype(jnp.bfloat16)
    outgoing = jnp.dot(chooser, tokens, preferred_element_type=jnp.float32).astype(jnp.bfloat16)
    outgoing = outgoing.reshape(columns, local_count * capacity, width)
    arrived = lax.all_to_all(outgoing, "col", split_axis=0, concat_axis=0, tiled=True)
    block_rows = lax.all_gather(arrived[None], "row", axis=0, tiled=True)
    count = block_rows.shape[0]
    grouped = block_rows.reshape(count, columns, local_count, capacity, width)
    expert = 0
    inputs = grouped[:, :, expert].reshape(-1, width)
    gate_part = jnp.dot(inputs, w_gate[expert], preferred_element_type=jnp.float32)
    up_part = jnp.dot(inputs, w_up[expert], preferred_element_type=jnp.float32)
    hidden = (jax.nn.silu(gate_part) * up_part).astype(jnp.bfloat16)
    outputs = hidden.reshape(count, columns, 1, capacity, unit_count)
    hidden_all = outputs.reshape(count, columns, local_count * capacity, unit_count)
    hidden_split = hidden_all.reshape(groups, columns, local_count, capacity, unit_count)
    piece = lax.all_gather(hidden_split, "row", axis=4, tiled=True)
    count = piece.shape[4]
    expert = 0
    rows = piece[:, :, expert].reshape(-1, count)
    block = w_down[expert]
    parts = [jnp.dot(rows, block, preferred_element_type=jnp.float32)]
    summed = jnp.stack(parts)
    expert_out = summed.astype(jnp.bfloat16).reshape(
        local_count, groups, columns, capacity, quarter
    )
    expert_out = jnp.transpose(expert_out, (1, 2, 0, 3, 4)).reshape(
        groups, columns, local_count * capacity, quarter
    )
    colwise = lax.all_to_all(expert_out, "col", split_axis=1, concat_axis=1, tiled=True)
    home = lax.all_to_all(colwise, "row", split_axis=0, concat_axis=3, tiled=True)
    results = home.reshape(experts * capacity, width)
    shares = gate_weights / jnp.sum(gate_weights, axis=1, keepdims=True)
    picked = results[slot_ids].astype(jnp.float32)
    combined = jnp.sum(shares[:, :, None] * picked, axis=1)
    return combined.astype(jnp.bfloat16)


def solution(mesh):
    placed = (
        P(("row", "col"), None),
        P(("row", "col"), None),
        P(("row", "col"), None),
        P("col", None, "row"),
        P("col", None, "row"),
        P("col", None, "row"),
    )
    return jax.shard_map(
        local, mesh=mesh, in_specs=placed, out_specs=P(("row", "col"), None), check_vma=False
    )
```

profile of v0, /device:TPU:1, one launch (start us, length us, event | category | flops | bytes accessed | tf_op | source)
XLA Modules:
  0.0 528.3 jit_solution(9375818899468450079)
XLA Ops:
  6.5 0.0 copy-start
  6.5 0.0 all-gather.6.cloned.1.call-start
  6.5 0.9 copy.41
  7.5 0.1 eq.43
  7.6 0.1 eq.39
  7.8 0.6 reduce-window.6
  8.4 0.2 slice_reduce_fusion
  8.6 0.1 fusion.10
  8.7 0.1 reduce_sum.31
  8.9 0.1 copy.44
  8.9 0.7 compare_select_fusion
  9.7 3.6 convolution_convert_fusion
  13.3 4.7 reshape.38
  18.0 107.6 %all_to_all.25 = bf16[64,5,4096]{2,1,0:T(8,128)(2,1)S(1)} all-to-all(bf16[64,5,4096]{2,1,0:T(8,128)(2,1)} %reshape.38), channel_id=1, replica_groups=mesh['row'=4,'col'=64] {'col'}, dimensions={0} | all-to-all | bytes 5242880 | tf_op jit(solution)/shard_map/all_to_all | solution.py:28
  125.6 3.2 copy.45
  128.8 0.0 all-gather.6.cloned.1.call-update
  128.8 0.3 all-gather.4.cloned.1.call-start
  129.2 101.0 %all-gather.6.cloned.1.call-done = bf16[256,5,4096]{2,0,1:T(8,128)(2,1)} async-done(((bf16[64,5,4096]{2,0,1:T(8,128)(2,1)}), bf16[256,5,4096]{2,0,1:T(8,128)(2,1)}) %all-gather.6.cloned.1.call-update) | async-done | bytes 10485776 | tf_op jit(solution)/shard_map/all_gather | solution.py:29
  230.2 15.2 %copy.46 = bf16[256,5,4096]{2,1,0:T(8,128)(2,1)} copy(bf16[256,5,4096]{2,0,1:T(8,128)(2,1)} %all-gather.6.cloned.1.call-done) | data formatting | bytes 20971520 | tf_op jit(solution)/shard_map/all_gather | solution.py:29
  245.4 16.8 %reshape_squeeze_reshape.3 = bf16[1280,4096]{1,0:T(8,128)(2,1)} reshape(bf16[256,5,4096]{2,1,0:T(8,128)(2,1)} %copy.46) | data formatting | bytes 20971520 | tf_op jit(solution)/shard_map/reshape;squeeze;reshape | solution.py:33
  262.3 0.0 copy-start.1
  262.3 0.0 copy-start.3
  262.3 9.3 %fusion.2 = f32[1280,384]{1,0:T(8,128)S(1)} fusion(bf16[1280,4096]{1,0:T(8,128)(2,1)} %reshape_squeeze_reshape.3, bf16[1,4096,384]{2,1,0:T(8,128)(2,1)} %param.9), kind=kOutput, calls=%fused_computation.7 | convolution fusion | flops 4026531840 | bytes 15597568 | tf_op jit(solution)/shard_map/dot_general | solution.py:34
  271.6 0.0 copy-done.1
  271.6 0.0 copy-done.3
  271.6 6.9 %fusion.4 = bf16[1280,384]{1,0:T(8,128)(2,1)} fusion(bf16[1280,4096]{1,0:T(8,128)(2,1)S(1)} %copy-done.1, bf16[1,4096,384]{2,1,0:T(8,128)(2,1)S(1)} %copy-done.3, f32[1280,384]{1,0:T(8,128)S(1)} %fusion.2), kind=kOutput, calls=%fused_computation.9 | convolution fusion | flops 4029480960 | bytes 16580608 | tf_op jit(solution)/shard_map/dot_general | solution.py:35
  278.6 3.0 reshape_reshape_reshape.3
  281.5 0.0 all-gather.4.cloned.1.call-update
  281.5 69.4 %all-gather.4.cloned.1.call-done = bf16[4,64,1,5,1536]{4,3,1,0,2:T(8,128)(2,1)} async-done(((bf16[4,64,1,5,384]{4,3,1,0,2:T(8,128)(2,1)}), bf16[4,64,1,5,1536]{4,3,1,0,2:T(8,128)(2,1)}) %all-gather.4.cloned.1.call-update) | async-done | bytes 3932176 | tf_op jit(solution)/shard_map/all_gather | solution.py:40
  351.0 7.6 %reshape_squeeze.3 = bf16[1280,1536]{1,0:T(8,128)(2,1)} reshape(bf16[4,64,1,5,1536]{4,3,1,0,2:T(8,128)(2,1)} %all-gather.4.cloned.1.call-done) | data formatting | bytes 7864320 | tf_op jit(solution)/shard_map/reshape;squeeze | solution.py:43
  358.6 0.0 copy-done
  358.6 7.6 %convolution_convert_fusion.1 = bf16[1280,1024]{1,0:T(8,128)(2,1)} fusion(bf16[1280,1536]{1,0:T(8,128)(2,1)} %reshape_squeeze.3, bf16[1,1536,1024]{2,1,0:T(8,128)(2,1)S(1)} %copy-done), kind=kOutput, calls=%fused_computation.3 | convolution fusion | flops 4027842560 | bytes 9699328 | tf_op jit(solution)/shard_map/dot_general | solution.py:45
  366.2 6.5 %reshape_transpose_reshape.3 = bf16[4,64,5,1024]{3,2,1,0:T(8,128)(2,1)} reshape(bf16[1280,1024]{1,0:T(8,128)(2,1)} %convolution_convert_fusion.1) | data formatting | bytes 5242880 | tf_op jit(solution)/shard_map/reshape;transpose;reshape | solution.py:50
  372.8 7.3 %copy.47 = bf16[4,64,5,1024]{3,0,2,1:T(4,128)(2,1)S(1)} copy(bf16[4,64,5,1024]{3,2,1,0:T(8,128)(2,1)} %reshape_transpose_reshape.3) | data formatting | bytes 5242880 | tf_op jit(solution)/shard_map/reshape;transpose;reshape | solution.py:50
  380.1 73.2 %all_to_all.26 = bf16[4,64,5,1024]{3,0,2,1:T(4,128)(2,1)S(1)} all-to-all(bf16[4,64,5,1024]{3,0,2,1:T(4,128)(2,1)S(1)} %copy.47), channel_id=1, replica_groups=mesh['row'=4,'col'=64] {'col'}, dimensions={1} | all-to-all | bytes 5242880 | tf_op jit(solution)/shard_map/all_to_all | solution.py:53
  453.3 2.3 copy.48
  455.6 0.0 copy-start.2
  455.7 4.8 all-to-all-start.2
  460.5 0.1 copy.50
  460.6 0.1 reshape.42
  460.8 0.0 copy-done.2
  460.8 0.1 copy.40
  460.9 31.4 %all-to-all-done.2 = bf16[4,64,5,1024]{3,1,2,0:T(8,128)(2,1)} async-done(((bf16[4,64,5,1024]{3,1,2,0:T(8,128)(2,1)}), bf16[4,64,5,1024]{3,1,2,0:T(8,128)(2,1)}, u32[]{:S(2)}, u32[]{:S(2)}) %all-to-all-start.2) | async-done | bytes 2621472 | tf_op jit(solution)/shard_map/all_to_all | solution.py:54
  492.3 3.8 copy.49
  496.0 2.6 copy.52
  498.7 7.3 %gather_fusion = bf16[256,4096]{1,0:T(8,128)(2,1)} fusion(bf16[320,4096]{1,0:T(8,128)(2,1)} %bitcast.43, s32[1024]{0:T(1024)S(1)} %pad_clamp_fusion), kind=kCustom, calls=%fused_computation | custom fusion | bytes 4195328 | tf_op jit(solution)/shard_map/gather | solution.py:57
  506.0 5.6 %reshape.52 = f32[128,2,4096]{2,1,0:T(2,128)} reshape(bf16[256,4096]{1,0:T(8,128)(2,1)} %gather_fusion) | data formatting | bytes 6291456 | tf_op jit(solution)/shard_map/convert_element_type | solution.py:57
  511.6 9.6 %multiply_reduce_fusion = bf16[128,4096]{1,0:T(8,128)(2,1)} fusion(f32[128,2,4096]{2,1,0:T(2,128)} %reshape.52, f32[128,2]{1,0:T(8,128)S(1)} %copy.40), kind=kLoop, calls=%fused_computation.2 | loop fusion | flops 1572864 | bytes 5243904 | tf_op jit(solution)/shard_map/reduce_sum | solution.py:58
  (7 shorter events, 0.1 us)
Async XLA Ops:
  6.5 352.1 %copy-start = (bf16[1,1536,1024]{2,1,0:T(8,128)(2,1)S(1)}, bf16[1,1536,1024]{2,1,0:T(8,128)(2,1)}, u32[]{:S(2)}) copy-start(bf16[1,1536,1024]{2,1,0:T(8,128)(2,1)} %param.11) | copy-start | bytes 9437188
  6.5 223.7 %all-gather.6.cloned.1.call-start = ((), (), s32[]{:S(2)}) async-start(), calls=%async_computation.4 | async-start | bytes 13107200 | tf_op jit(solution)/shard_map/all_gather | solution.py:29
  128.8 222.1 %all-gather.4.cloned.1.call-start = ((), (), s32[]{:S(2)}) async-start(), calls=%async_computation.3 | async-start | bytes 7864320 | tf_op jit(solution)/shard_map/all_gather | solution.py:40
  262.3 9.4 %copy-start.1 = (bf16[1280,4096]{1,0:T(8,128)(2,1)S(1)}, bf16[1280,4096]{1,0:T(8,128)(2,1)}, u32[]{:S(2)}) copy-start(bf16[1280,4096]{1,0:T(8,128)(2,1)} %reshape_squeeze_reshape.3) | copy-start | bytes 31457284
  262.3 9.4 %copy-start.3 = (bf16[1,4096,384]{2,1,0:T(8,128)(2,1)S(1)}, bf16[1,4096,384]{2,1,0:T(8,128)(2,1)}, u32[]{:S(2)}) copy-start(bf16[1,4096,384]{2,1,0:T(8,128)(2,1)} %param.10) | copy-start | bytes 9437188
  455.6 5.1 copy-start.2
  455.7 36.6 %all-to-all-start.2 = ((bf16[4,64,5,1024]{3,1,2,0:T(8,128)(2,1)}), bf16[4,64,5,1024]{3,1,2,0:T(8,128)(2,1)}, u32[]{:S(2)}, u32[]{:S(2)}) async-start(bf16[4,64,5,1024]{3,1,2,0:T(8,128)(2,1)} %copy.48), calls=%async_computation.2 | async-start | bytes 5242880 | tf_op jit(solution)/shard_map/all_to_all | solution.py:54
Sparse Core Ops, SparseCore 0:
  128.9 101.2 all-gather.5
  281.7 69.2 all-gather.3
where the time goes:
time: 534 us; the launch traced here: 528 us
  waiting for transfers between devices  202 us (38%)
  blocking collectives  181 us (34%)
  local copies, waits for them, and re-layouts  88.1 us (16%)
  matrix products  27.4 us (5%)
  between operations  13.7 us (3%)
  other arithmetic  11.2 us (2%)
    all_to_all x1, blocking collectives, local(): lax.all_to_all(outgoing, 'col', split_axis=0, concat_axis=0, tiled=True)  108 us
    all_gather x1, waiting for transfers between devices, local(): block_rows = lax.all_gather(arrived[None], 'row', axis=0, tiled=True)  101 us
    all_to_all x1, blocking collectives, local(): lax.all_to_all(expert_out, 'col', split_axis=1, concat_axis=1, tiled=True)  73.2 us
    all_gather x1, waiting for transfers between devices, local(): piece = lax.all_gather(hidden_split, 'row', axis=4, tiled=True)  69.4 us
    all_to_all x1, waiting for transfers between devices, local(): lax.all_to_all(colwise, 'row', split_axis=0, concat_axis=3, tiled=True)  31.4 us
    another operation x1, local copies, waits for them, and re-layouts, local(): inputs = grouped[:, :, expert].reshape(-1, width)  16.8 us
    all_gather x1, local copies, waits for them, and re-layouts, local(): block_rows = lax.all_gather(arrived[None], 'row', axis=0, tiled=True)  15.2 us
    another operation x2, local copies, waits for them, and re-layouts, local(): jnp.transpose(expert_out, (1, 2, 0, 3, 4))  13.9 us
  transfers between devices with their start and end apart: 3, of which 3 were waited for; matrix products, arithmetic and copies ran while one was open for 0% of the time, Pallas kernels for 0%

commit v1 on v0

--- a/solution.py
+++ b/solution.py
@@ -37,7 +37,9 @@
     outputs = hidden.reshape(count, columns, 1, capacity, unit_count)
     hidden_all = outputs.reshape(count, columns, local_count * capacity, unit_count)
     hidden_split = hidden_all.reshape(groups, columns, local_count, capacity, unit_count)
-    piece = lax.all_gather(hidden_split, "row", axis=4, tiled=True)
+    piece = jnp.concatenate(
+        lax.all_to_all(jnp.stack([hidden_split] * lax.axis_size("row")), "row", 0, 0), axis=4
+    )
     count = piece.shape[4]
     expert = 0
     rows = piece[:, :, expert].reshape(-1, count)

time: 534 us -> 509 us (0.953)
  waiting for transfers between devices: 202 us -> 133 us
  blocking collectives: 181 us -> 231 us
    all_gather x1 -> x0, waiting for transfers between devices: 69.4 us -> none  [local(): piece = lax.all_gather(hidden_split, 'row', axis=4, tiled=True)]
    all_to_all x0 -> x1, blocking collectives: none -> 49.1 us  [local(): lax.all_to_all(jnp.stack([hidden_split] * lax.axis_size('row')), 'row', 0...]
    another operation x3 -> x4, local copies, waits for them, and re-layouts: 10.6 us -> 5.23 us  [the longest x3 5.23 us: local(): jnp.stack([hidden_split] * lax.axis_size('row'))]
  transfers between devices with their start and end apart: 3 -> 2, of which waited for: 3 -> 2; matrix products, arithmetic and copies ran while one was open for 0% -> 0% of each run, Pallas kernels for 0% -> 0%
where the time goes in v1:
time: 509 us; the launch traced here: 505 us
  blocking collectives  231 us (45%)
  waiting for transfers between devices  133 us (26%)
  local copies, waits for them, and re-layouts  86 us (17%)
  matrix products  25.4 us (5%)
  between operations  13.8 us (3%)
  other arithmetic  11.2 us (2%)
    all_to_all x1, blocking collectives, local(): lax.all_to_all(outgoing, 'col', split_axis=0, concat_axis=0, tiled=True)  108 us
    all_gather x1, waiting for transfers between devices, local(): block_rows = lax.all_gather(arrived[None], 'row', axis=0, tiled=True)  101 us
    all_to_all x1, blocking collectives, local(): lax.all_to_all(expert_out, 'col', split_axis=1, concat_axis=1, tiled=True)  74.4 us
    all_to_all x1, blocking collectives, local(): lax.all_to_all(jnp.stack([hidden_split] * lax.axis_size('row')), 'row', 0...  49.1 us
    all_to_all x1, waiting for transfers between devices, local(): lax.all_to_all(colwise, 'row', split_axis=0, concat_axis=3, tiled=True)  31.4 us
    another operation x1, local copies, waits for them, and re-layouts, local(): inputs = grouped[:, :, expert].reshape(-1, width)  16.8 us
    all_gather x1, local copies, waits for them, and re-layouts, local(): block_rows = lax.all_gather(arrived[None], 'row', axis=0, tiled=True)  15.2 us
    another operation x2, local copies, waits for them, and re-layouts, local(): jnp.transpose(expert_out, (1, 2, 0, 3, 4))  13.4 us
  transfers between devices with their start and end apart: 2, of which 2 were waited for; matrix products, arithmetic and copies ran while one was open for 0% of the time, Pallas kernels for 0%

profile of v1, /device:TPU:1, one launch (start us, length us, event | category | flops | bytes accessed | tf_op | source)
XLA Modules:
  0.0 505.1 jit_solution(18416693582367651686)
XLA Ops:
  6.5 0.0 copy-start
  6.5 0.0 all-gather.3.cloned.1.call-start
  6.5 0.9 copy.57
  7.5 0.1 eq.43
  7.6 0.1 eq.39
  7.8 0.6 reduce-window.6
  8.4 0.2 slice_reduce_fusion
  8.6 0.1 fusion.10
  8.7 0.1 reduce_sum.31
  8.9 0.1 copy.60
  8.9 0.7 compare_select_fusion
  9.7 3.6 convolution_convert_fusion
  13.3 4.7 reshape.45
  18.0 107.9 %all_to_all.30 = bf16[64,5,4096]{2,1,0:T(8,128)(2,1)S(1)} all-to-all(bf16[64,5,4096]{2,1,0:T(8,128)(2,1)} %reshape.45), channel_id=1, replica_groups=mesh['row'=4,'col'=64] {'col'}, dimensions={0} | all-to-all | bytes 5242880 | tf_op jit(solution)/shard_map/all_to_all | solution.py:28
  125.8 3.2 copy.61
  129.1 0.0 all-gather.3.cloned.1.call-update
  129.1 101.4 %all-gather.3.cloned.1.call-done = bf16[256,5,4096]{2,0,1:T(8,128)(2,1)} async-done(((bf16[64,5,4096]{2,0,1:T(8,128)(2,1)}), bf16[256,5,4096]{2,0,1:T(8,128)(2,1)}) %all-gather.3.cloned.1.call-update) | async-done | bytes 10485776 | tf_op jit(solution)/shard_map/all_gather | solution.py:29
  230.5 15.2 %copy.62 = bf16[256,5,4096]{2,1,0:T(8,128)(2,1)} copy(bf16[256,5,4096]{2,0,1:T(8,128)(2,1)} %all-gather.3.cloned.1.call-done) | data formatting | bytes 20971520 | tf_op jit(solution)/shard_map/all_gather | solution.py:29
  245.7 16.8 %reshape_squeeze_reshape.6 = bf16[1280,4096]{1,0:T(8,128)(2,1)} reshape(bf16[256,5,4096]{2,1,0:T(8,128)(2,1)} %copy.62) | data formatting | bytes 20971520 | tf_op jit(solution)/shard_map/reshape;squeeze;reshape | solution.py:33
  262.6 0.0 copy-start.1
  262.6 0.0 copy-start.3
  262.6 9.3 %fusion.2 = f32[1280,384]{1,0:T(8,128)S(1)} fusion(bf16[1280,4096]{1,0:T(8,128)(2,1)} %reshape_squeeze_reshape.6, bf16[1,4096,384]{2,1,0:T(8,128)(2,1)} %param.9), kind=kOutput, calls=%fused_computation.7 | convolution fusion | flops 4026531840 | bytes 15597568 | tf_op jit(solution)/shard_map/dot_general | solution.py:34
  271.9 0.0 copy-done.1
  271.9 0.0 copy-done.3
  271.9 6.9 %fusion.4 = bf16[1280,384]{1,0:T(8,128)(2,1)} fusion(bf16[1280,4096]{1,0:T(8,128)(2,1)S(1)} %copy-done.1, bf16[1,4096,384]{2,1,0:T(8,128)(2,1)S(1)} %copy-done.3, f32[1280,384]{1,0:T(8,128)S(1)} %fusion.2), kind=kOutput, calls=%fused_computation.9 | convolution fusion | flops 4029480960 | bytes 16580608 | tf_op jit(solution)/shard_map/dot_general | solution.py:35
  278.8 3.0 stack_reshape_reshape_reshape.2
  281.8 1.6 copy.63
  283.4 0.7 stack.4
  284.1 49.1 %all_to_all.31 = bf16[4,4,64,1,5,384]{5,2,4,3,1,0:T(8,128)(2,1)S(1)} all-to-all(bf16[4,4,64,1,5,384]{5,2,4,3,1,0:T(8,128)(2,1)S(1)} %stack.4), channel_id=1, replica_groups=mesh['row'=4,'col'=64] {'row'}, dimensions={0} | all-to-all | bytes 7864320 | tf_op jit(solution)/shard_map/all_to_all | solution.py:41
  333.2 3.0 copy.64
  336.3 0.7 copy.70
  337.0 0.0 copy-done
  337.0 5.5 %convolution_convert_fusion.1 = bf16[1280,1024]{1,0:T(8,128)(2,1)} fusion(bf16[1280,1536]{1,0:T(8,128)(2,1)S(1)} %bitcast.50, bf16[1,1536,1024]{2,1,0:T(8,128)(2,1)S(1)} %copy-done), kind=kOutput, calls=%fused_computation.3 | convolution fusion | flops 4027842560 | bytes 9699328 | tf_op jit(solution)/shard_map/dot_general | solution.py:47
  342.5 6.0 %reshape_transpose_reshape.3 = bf16[4,64,5,1024]{3,2,1,0:T(8,128)(2,1)} reshape(bf16[1280,1024]{1,0:T(8,128)(2,1)} %convolution_convert_fusion.1) | data formatting | bytes 5242880 | tf_op jit(solution)/shard_map/reshape;transpose;reshape | solution.py:52
  348.5 7.3 %copy.65 = bf16[4,64,5,1024]{3,0,2,1:T(4,128)(2,1)S(1)} copy(bf16[4,64,5,1024]{3,2,1,0:T(8,128)(2,1)} %reshape_transpose_reshape.3) | data formatting | bytes 5242880 | tf_op jit(solution)/shard_map/reshape;transpose;reshape | solution.py:52
  355.9 74.4 %all_to_all.32 = bf16[4,64,5,1024]{3,0,2,1:T(4,128)(2,1)S(1)} all-to-all(bf16[4,64,5,1024]{3,0,2,1:T(4,128)(2,1)S(1)} %copy.65), channel_id=1, replica_groups=mesh['row'=4,'col'=64] {'col'}, dimensions={1} | all-to-all | bytes 5242880 | tf_op jit(solution)/shard_map/all_to_all | solution.py:55
  430.2 2.3 copy.66
  432.6 4.7 all-to-all-start.3
  437.3 0.1 copy.68
  437.4 0.1 reshape.50
  437.5 0.0 copy-done.2
  437.6 0.1 copy.56
  437.7 31.4 %all-to-all-done.3 = bf16[4,64,5,1024]{3,1,2,0:T(8,128)(2,1)} async-done(((bf16[4,64,5,1024]{3,1,2,0:T(8,128)(2,1)}), bf16[4,64,5,1024]{3,1,2,0:T(8,128)(2,1)}, u32[]{:S(2)}, u32[]{:S(2)}) %all-to-all-start.3) | async-done | bytes 2621472 | tf_op jit(solution)/shard_map/all_to_all | solution.py:56
  469.1 3.8 copy.67
  472.8 2.6 copy.71
  475.5 7.3 %gather_fusion = bf16[256,4096]{1,0:T(8,128)(2,1)} fusion(bf16[320,4096]{1,0:T(8,128)(2,1)} %bitcast.46, s32[1024]{0:T(1024)S(1)} %pad_clamp_fusion), kind=kCustom, calls=%fused_computation | custom fusion | bytes 4195328 | tf_op jit(solution)/shard_map/gather | solution.py:59
  482.8 5.6 %reshape.60 = f32[128,2,4096]{2,1,0:T(2,128)} reshape(bf16[256,4096]{1,0:T(8,128)(2,1)} %gather_fusion) | data formatting | bytes 6291456 | tf_op jit(solution)/shard_map/convert_element_type | solution.py:59
  488.4 9.6 %multiply_reduce_fusion = bf16[128,4096]{1,0:T(8,128)(2,1)} fusion(f32[128,2,4096]{2,1,0:T(2,128)} %reshape.60, f32[128,2]{1,0:T(8,128)S(1)} %copy.56), kind=kLoop, calls=%fused_computation.2 | loop fusion | flops 1572864 | bytes 5243904 | tf_op jit(solution)/shard_map/reduce_sum | solution.py:60
  (8 shorter events, 0.1 us)
Async XLA Ops:
  6.5 330.4 %copy-start = (bf16[1,1536,1024]{2,1,0:T(8,128)(2,1)S(1)}, bf16[1,1536,1024]{2,1,0:T(8,128)(2,1)}, u32[]{:S(2)}) copy-start(bf16[1,1536,1024]{2,1,0:T(8,128)(2,1)} %param.11) | copy-start | bytes 9437188
  6.5 224.0 %all-gather.3.cloned.1.call-start = ((), (), s32[]{:S(2)}) async-start(), calls=%async_computation.4 | async-start | bytes 13107200 | tf_op jit(solution)/shard_map/all_gather | solution.py:29
  262.6 9.4 %copy-start.1 = (bf16[1280,4096]{1,0:T(8,128)(2,1)S(1)}, bf16[1280,4096]{1,0:T(8,128)(2,1)}, u32[]{:S(2)}) copy-start(bf16[1280,4096]{1,0:T(8,128)(2,1)} %reshape_squeeze_reshape.6) | copy-start | bytes 31457284
  262.6 9.4 %copy-start.3 = (bf16[1,4096,384]{2,1,0:T(8,128)(2,1)S(1)}, bf16[1,4096,384]{2,1,0:T(8,128)(2,1)}, u32[]{:S(2)}) copy-start(bf16[1,4096,384]{2,1,0:T(8,128)(2,1)} %param.10) | copy-start | bytes 9437188
  432.6 4.9 copy-start.2
  432.6 36.5 %all-to-all-start.3 = ((bf16[4,64,5,1024]{3,1,2,0:T(8,128)(2,1)}), bf16[4,64,5,1024]{3,1,2,0:T(8,128)(2,1)}, u32[]{:S(2)}, u32[]{:S(2)}) async-start(bf16[4,64,5,1024]{3,1,2,0:T(8,128)(2,1)} %copy.66), calls=%async_computation.3 | async-start | bytes 5242880 | tf_op jit(solution)/shard_map/all_to_all | solution.py:56
Sparse Core Ops, SparseCore 0:
  129.2 101.2 all-gather.2
